TPU v7x, 256 devices: a whole 4x4x8 slice. The times are simulated.
256 devices in a mesh: seq: 32 (over x, z), tp: 8 (over y, core).
Axes of the slice: x: 4, y: 4, z: 8, core: 2. Of those that a mesh axis runs over, the one named last changes fastest.
Arguments:
- tokens: bfloat16 [32768, 2048], P('seq', 'tp'), may hold values from -6 to 6
- w_inner: bfloat16 [2048, 2, 4096], P('seq', None, 'tp'), may hold values from -0.125 to 0.125
- w_states: bfloat16 [2048, 256], P('seq'), may hold values from -0.125 to 0.125
- w_step: bfloat16 [2048, 64], P('seq', 'tp'), may hold values from -0.125 to 0.125
- conv_inner: float32 [4, 4096], P(None, 'tp'), may hold values from -3 to 3
- conv_states: float32 [4, 256], replicated, may hold values from -3 to 3
- decay_rate: float32 [64], P('tp'), may hold values from 0 to 1, as said below
- step_bias: float32 [64], P('tp'), may hold values from -1 to 0.5
- skip_gain: float32 [64], P('tp'), may hold values from 0.5 to 1.5
- norm_gain: float32 [4096], P('tp'), may hold values from 0.5 to 1.5
- w_output: bfloat16 [4096, 2048], P('tp', 'seq'), may hold values from -0.09375 to 0.09375
- block_owner: int32 [128], replicated, may hold values from 0 to 19, as said below
- lengths: int32 [20], replicated, may hold values from 1 to 16384, as said below
Outputs:
- mixed: bfloat16 [32768, 2048], P('seq', 'tp')
Inputs may be any that keep to these rules, and one draw needn't show every extreme that they name: `block_owner`: each prompt's blocks are consecutive, prompt r has ceil(lengths[r] / 256) of them, and the prompts follow one another in an order drawn afresh; one prompt has 64 blocks and is neither the first nor the last in that order. `lengths`: one prompt has exactly 16384 tokens. `decay_rate`: Positive.
All inputs are finite; a program needn't handle non-finite values.
Results may differ from a plain program's by a relative error of at most 0.0075.
Values may be sent and summed in bfloat16 or wider, within the bound.
No kernel may reach another device: no remote copies, remote signals or barrier semaphores. Data moves between devices by JAX's collectives and lax.ppermute only.
A program may use at most 64 MiB of HBM per device.

v0:
```python
import jax
import jax.numpy as jnp
from jax import lax
from jax.sharding import Mesh
from jax.sharding import PartitionSpec as P

BLOCK = 256
LONGEST = 64
SEQ = ("sx", "sz")
SEQ_INNER = 8


def passed_along(value, axis, by):
    count = lax.axis_size(axis)
    pairs = [(i, i + by) for i in range(count) if 0 <= i + by < count]
    return lax.ppermute(value, axis, pairs)


def convolve(values, edge_rows, weights, in_block, carry_on):
    lag_rows = weights.shape[0] - 1
    row_total = values.shape[0]
    widened = jnp.concatenate([edge_rows, values], axis=0).astype(jnp.float32)
    total = jnp.zeros(values.shape, jnp.float32)
    for offset in range(weights.shape[0]):
        shifted = widened[lag_rows - offset : lag_rows - offset + row_total]
        keeping = (in_block >= offset) | carry_on
        total = total + jnp.where(keeping[:, None], shifted, 0.0) * weights[offset]
    return jax.nn.silu(total).astype(jnp.bfloat16)


def on_device(
    tokens,
    w_inner,
    w_states,
    w_step,
    conv_inner,
    conv_states,
    decay_rate,
    step_bias,
    skip_gain,
    norm_gain,
    w_output,
    block_owner,
    lengths,
):
    row_count = tokens.shape[0]
    local_blocks = row_count // BLOCK
    total_blocks = block_owner.shape[0]
    heads_here = w_step.shape[1]
    inner_here = w_inner.shape[2]
    state_size = w_states.shape[1] // 2
    head_size = inner_here // heads_here
    lag_rows = conv_inner.shape[0] - 1
    block_ids = jnp.arange(total_blocks, dtype=jnp.int32)
    same_owner = block_owner[:, None] == block_owner[None, :]
    first_block = jnp.min(jnp.where(same_owner, block_ids[None, :], total_blocks), axis=1)
    starting = (first_block == block_ids).astype(jnp.int32)
    request_ids = jnp.arange(lengths.shape[0], dtype=jnp.int32)
    own_length = jnp.sum(
        jnp.where(block_owner[:, None] == request_ids[None, :], lengths[None, :], 0), axis=1
    )
    valid_rows = jnp.clip(own_length - (block_ids - first_block) * BLOCK, 0, BLOCK)
    seq_index = lax.axis_index(SEQ)
    local_start = lax.dynamic_slice_in_dim(starting, seq_index * local_blocks, local_blocks)
    local_valid = lax.dynamic_slice_in_dim(valid_rows, seq_index * local_blocks, local_blocks)
    in_block = jnp.arange(row_count, dtype=jnp.int32) % BLOCK
    carry_on = jnp.repeat(local_start == 0, BLOCK)
    whole = lax.all_gather(tokens, "tp", axis=1, tiled=True)
    local_rows = w_inner.shape[0]
    joined = jnp.concatenate(
        [w_inner.reshape(local_rows, 2 * inner_here), w_states, w_step], axis=1
    )
    weights = lax.all_gather(
        lax.all_gather(joined, "sz", axis=0, tiled=True), "sx", axis=0, tiled=True
    )
    all_sum = jnp.dot(whole, weights, preferred_element_type=jnp.float32)
    projected = all_sum.astype(jnp.bfloat16)
    gate_in = projected[:, :inner_here]
    x_in = projected[:, inner_here : 2 * inner_here]
    bc_in = projected[:, 2 * inner_here : 2 * inner_here + 2 * state_size]
    step_raw = projected[:, 2 * inner_here + 2 * state_size :]
    edge_inner, edge_states = passed_along(
        (x_in[row_count - lag_rows :], bc_in[row_count - lag_rows :]), SEQ, 1
    )
    x_conv = convolve(x_in, edge_inner, conv_inner, in_block, carry_on)
    bc_conv = convolve(bc_in, edge_states, conv_states, in_block, carry_on)
    step_size = jax.nn.softplus(step_raw.astype(jnp.float32) + step_bias)
    log_decay = -decay_rate * step_size
    x_heads = x_conv.reshape(local_blocks, BLOCK, heads_here, head_size)
    b_rows = bc_conv[:, :state_size].reshape(local_blocks, BLOCK, state_size)
    c_rows = bc_conv[:, state_size:].reshape(local_blocks, BLOCK, state_size)
    step_blocks = step_size.reshape(local_blocks, BLOCK, heads_here)
    cumulative = jnp.cumsum(log_decay.reshape(local_blocks, BLOCK, heads_here), axis=1)
    causal = jnp.arange(BLOCK)[:, None] >= jnp.arange(BLOCK)[None, :]
    spread = cumulative[:, :, None, :] - cumulative[:, None, :, :]
    decays = jnp.exp(jnp.where(causal[None, :, :, None], spread, -jnp.inf))
    intersection = jnp.einsum("cin,cjn->cij", c_rows, b_rows, preferred_element_type=jnp.float32)
    mixing = (decays * intersection[:, :, :, None] * step_blocks[:, None, :, :]).astype(
        jnp.bfloat16
    )
    y_inner = jnp.einsum("cijh,cjhp->cihp", mixing, x_heads, preferred_element_type=jnp.float32)
    final_log = cumulative[:, -1, :]
    tail_weight = jnp.exp(final_log[:, None, :] - cumulative) * step_blocks
    weighted_b = (tail_weight[:, :, :, None] * b_rows.astype(jnp.float32)[:, :, None, :]).astype(
        jnp.bfloat16
    )
    fresh = jnp.einsum("cjhn,cjhp->chnp", weighted_b, x_heads, preferred_element_type=jnp.float32)
    keep_flag = jnp.where(local_start == 1, 0.0, 1.0).astype(jnp.float32)
    block_gain_each = jnp.exp(final_log) * keep_flag[:, None]

    def fold_block(carry, item):
        gain_now, fresh_now = item
        return ((carry[0] * gain_now, gain_now[:, None, None] * carry[1] + fresh_now), None)

    zero_state = jnp.zeros((heads_here, state_size, head_size), jnp.float32)
    unit_gain = jnp.ones((heads_here,), jnp.float32)
    (block_gain, block_state), _ = lax.scan(
        fold_block, (unit_gain, zero_state), (block_gain_each, fresh)
    )

    def packed(gain, state):
        rows = jnp.broadcast_to(gain[:, None, None], (heads_here, 1, head_size))
        return jnp.concatenate([state, rows], axis=1)

    prefix = passed_along(packed(block_gain, block_state), SEQ, 1)
    needed = min(-(-(LONGEST - 1) // local_blocks), lax.axis_size(SEQ) - 1)
    reach = 1
    while reach < needed:
        earlier = passed_along(prefix, SEQ, reach)
        gain_now = prefix[:, state_size:, :1]
        prefix = jnp.concatenate(
            [
                gain_now * earlier[:, :state_size] + prefix[:, :state_size],
                gain_now * earlier[:, state_size:],
            ],
            axis=1,
        )
        reach *= 2
    entering = prefix[:, :state_size]

    def pass_block(previous, item):
        log_now, keep_now, fresh_now = item
        incoming = previous * keep_now
        return (jnp.exp(log_now)[:, None, None] * incoming + fresh_now, incoming)

    _, incoming_all = lax.scan(pass_block, entering, (final_log, keep_flag, fresh))
    incoming_half = incoming_all.astype(jnp.bfloat16)
    y_carry = jnp.exp(cumulative)[:, :, :, None] * jnp.einsum(
        "cin,chnp->cihp", c_rows, incoming_half, preferred_element_type=jnp.float32
    )
    y_total = (y_inner + y_carry).reshape(row_count, inner_here) + jnp.repeat(skip_gain, head_size)[
        None, :
    ] * x_conv.astype(jnp.float32)
    gated = y_total * jax.nn.silu(gate_in.astype(jnp.float32))
    squares = lax.psum(jnp.sum(gated * gated, axis=1), "tp")
    square_mean = squares / (inner_here * lax.axis_size("tp"))
    normed = (gated * lax.rsqrt(square_mean + 1e-05)[:, None] * norm_gain).astype(jnp.bfloat16)
    partial_out = jnp.dot(
        normed,
        lax.all_gather(
            lax.all_gather(w_output, "sz", axis=1, tiled=True), "sx", axis=1, tiled=True
        ),
        preferred_element_type=jnp.float32,
    )
    summed = lax.psum_scatter(partial_out, "tp", scatter_dimension=1, tiled=True)
    live = in_block < jnp.repeat(local_valid, BLOCK)
    return jnp.where(live[:, None], summed, 0.0).astype(jnp.bfloat16)


def solution(mesh):
    seq_count, tp_count = mesh.devices.shape
    split = Mesh(
        mesh.devices.reshape(seq_count // SEQ_INNER, SEQ_INNER, tp_count), ("sx", "sz", "tp")
    )
    return jax.shard_map(
        on_device,
        mesh=split,
        in_specs=(
            P(SEQ, "tp"),
            P(SEQ, None, "tp"),
            P(SEQ, None),
            P(SEQ, "tp"),
            P(None, "tp"),
            P(),
            P("tp"),
            P("tp"),
            P("tp"),
            P("tp"),
            P("tp", SEQ),
            P(),
            P(),
        ),
        out_specs=P(SEQ, "tp"),
        check_vma=False,
    )
```

profile of v0, /device:TPU:1, one launch (start us, length us, event | category | flops | bytes accessed | tf_op | source)
XLA Modules:
  0.0 449.6 jit_solution(2950230188887680185)
XLA Ops:
  8.3 1.4 pad_maximum_fusion.4
  10.6 38.2 %all-gather.5.cloned.1.call-done = bf16[512,1288]{1,0:T(8,128)(2,1)} async-done(((bf16[64,1288]{1,0:T(8,128)(2,1)}), bf16[512,1288]{1,0:T(8,128)(2,1)}) %all-gather.5.cloned.1.call-update) | async-done | bytes 1318928 | tf_op jit(solution)/shard_map/all_gather | solution.py:74
  49.8 42.1 %all-gather.9.cloned.1.call-done = bf16[1024,2048]{1,0:T(8,128)(2,1)} async-done(((bf16[1024,256]{1,0:T(8,128)(2,1)}), bf16[1024,2048]{1,0:T(8,128)(2,1)}) %all-gather.9.cloned.1.call-update) | async-done | bytes 4194320 | tf_op jit(solution)/shard_map/all_gather | solution.py:68
  91.9 66.0 %all-gather.7.cloned.1.call-done = bf16[2048,1288]{1,0:T(8,128)(2,1)} async-done(((bf16[512,1288]{1,0:T(8,128)(2,1)}), bf16[2048,1288]{1,0:T(8,128)(2,1)}) %all-gather.7.cloned.1.call-update) | async-done | bytes 5275664 | tf_op jit(solution)/shard_map/all_gather | solution.py:73
  157.9 9.6 %fusion.10 = bf16[1024,1288]{0,1:T(8,128)(2,1)S(1)} fusion(bf16[2048,1288]{1,0:T(8,128)(2,1)} %all-gather.7.cloned.1.call-done, bf16[1024,2048]{1,0:T(8,128)(2,1)} %all-gather.9.cloned.1.call-done), kind=kOutput, calls=%fused_computation.20 | convolution fusion | flops 5403582464 | bytes 12107776 | tf_op jit(solution)/shard_map/dot_general | solution.py:76
  167.8 3.2 collective-permute-start
  171.0 3.2 collective-permute-start.1
  174.3 2.3 reduce-window.6
  177.8 2.3 slice.159
  183.5 1.8 maximum_convert_fusion
  185.3 3.1 multiply_convert_fusion.5
  188.4 2.6 reshape.134
  191.0 4.9 %fusion.15 = f32[4,8,128,64]{3,2,1,0:T(8,128)} fusion(f32[4,256,128]{2,1,0:T(8,128)} %copy.83, f32[4,256,8]{1,2,0:T(8,128)S(1)} %exponential_multiply_fusion, bf16[4,256,8,64]{1,0,3,2:T(4,128)(2,1)} %reshape.134), kind=kOutput, calls=%fused_computation.27 | convolution fusion | flops 136314880 | bytes 2654208 | tf_op jit(solution)/shard_map/cjhn,cjhp->chnp/dot_general | solution.py:107
  195.9 4.8 %while.26 = (s32[]{:T(128)}, f32[8]{0:T(128)S(1)}, f32[8,128,64]{2,1,0:T(8,128)S(1)}, f32[4,8]{1,0:T(4,128)S(1)}, f32[4,8,128,64]{3,2,1,0:T(8,128)}, /*index=5*/s32[]{:T(128)}, s32[]{:T(128)}) while((s32[]{:T(128)}, f32[8]{0:T(128)S(1)}, f32[8,128,64]{2,1,0:T(8,128)S(1)}, f32[4,8]{1,0:T(4,128)S(1)}, f32[4,8,128,64]{3,2,1,0:T(8,128)}, ...), condition=%wide.region_5.6_spmd.clone, body=%wide.region_4.5_spmd.clone.sunk | while | flops 196627 | bytes 786688 | solution.py:117
  201.1 3.2 collective-permute-start.2
  204.3 9.8 %collective-permute-done.2 = f32[8,129,64]{1,2,0:T(8,128)S(1)} collective-permute-done((f32[8,129,64]{1,2,0:T(8,128)S(1)}, f32[8,129,64]{1,2,0:T(8,128)S(1)}, u32[]{:S(2)}, u32[]{:S(2)}) %collective-permute-start.2) | collective-permute-done | bytes 264224 | tf_op jit(solution)/shard_map/ppermute | solution.py:16
  214.1 4.4 collective-permute-start.3
  218.7 8.8 %collective-permute-done.3 = f32[8,129,64]{1,2,0:T(8,128)S(1)} collective-permute-done((f32[8,129,64]{1,2,0:T(8,128)S(1)}, f32[8,129,64]{1,2,0:T(8,128)S(1)}, u32[]{:S(2)}, u32[]{:S(2)}) %collective-permute-start.3) | collective-permute-done | bytes 264224 | tf_op jit(solution)/shard_map/ppermute | solution.py:16
  227.7 6.1 %collective-permute-start.4 = (f32[8,129,64]{1,2,0:T(8,128)S(1)}, f32[8,129,64]{1,2,0:T(8,128)S(1)}, u32[]{:S(2)}, u32[]{:S(2)}) collective-permute-start(f32[8,129,64]{1,2,0:T(8,128)S(1)} %pad_maximum_fusion.1), channel_id=1, source_target_pairs={{0,16},{8,24},{16,32},{24,40},{32,48},{40,56},{48,64},{56,72},{64,... | collective-permute-start | bytes 792584 | tf_op jit(solution)/shard_map/ppermute | solution.py:16
  234.0 21.2 %collective-permute-done.4 = f32[8,129,64]{1,2,0:T(8,128)S(1)} collective-permute-done((f32[8,129,64]{1,2,0:T(8,128)S(1)}, f32[8,129,64]{1,2,0:T(8,128)S(1)}, u32[]{:S(2)}, u32[]{:S(2)}) %collective-permute-start.4) | collective-permute-done | bytes 264224 | tf_op jit(solution)/shard_map/ppermute | solution.py:16
  256.8 9.3 %collective-permute-start.5 = (f32[8,129,64]{1,2,0:T(8,128)}, f32[8,129,64]{1,2,0:T(8,128)}, u32[]{:S(2)}, u32[]{:S(2)}) collective-permute-start(f32[8,129,64]{1,2,0:T(8,128)} %pad_maximum_fusion.2), channel_id=1, source_target_pairs={{0,32},{8,40},{16,48},{24,56},{32,64},{40,72},{48,80},{56,88},{64,... | collective-permute-start | bytes 792584 | tf_op jit(solution)/shard_map/ppermute | solution.py:16
  266.1 40.6 %all_gather.18 = bf16[512,512]{0,1:T(8,128)(2,1)} all-gather(bf16[512,64]{0,1:T(8,128)(2,1)S(1)} %copy-done.6), channel_id=1, replica_groups=mesh['sx'=4,'sz'=8,'tp'=8] {'sz'}, dimensions={1}, use_global_device_ids=true | all-gather | bytes 589824 | tf_op jit(solution)/shard_map/all_gather | solution.py:161
  311.8 4.0 collective-permute-start.6
  315.8 1.3 fusion.37
  317.2 4.5 collective-permute-done.6
  322.0 20.4 %while.25 = (s32[]{:T(128)}, f32[8,128,64]{2,1,0:T(8,128)S(1)}, bf16[4,8,128,64]{3,2,1,0:T(8,128)(2,1)}, f32[4,8]{1,0:T(4,128)}, f32[4]{0:T(128)}, /*index=5*/f32[4,8,128,64]{3,2,1,0:T(8,128)}, s32[]{:T(128)}) while((s32[]{:T(128)}, f32[8,128,64]{2,1,0:T(8,128)S(1)}, bf16[4,8,128,64]{3,2,1,0:T(8,128)(2,1)}, f32[4,8]{1,0:T(4,128)}, ...), condition=%wide.region_7.8_spmd, body=%wide.region_6.7_spmd.sunk | while | flops 262146 | bytes 1574085 | solution.py:146
  322.0 1.2 dynamic_slice.45
  323.2 1.4 bitcast_dynamic-update-slice_fusion.2
  325.3 1.8 bitcast_add_fusion.5
  327.2 1.2 dynamic_slice.45
  328.4 1.4 bitcast_dynamic-update-slice_fusion.2
  330.4 1.8 bitcast_add_fusion.5
  332.3 1.2 dynamic_slice.45
  333.5 1.4 bitcast_dynamic-update-slice_fusion.2
  335.5 1.8 bitcast_add_fusion.5
  337.4 1.2 dynamic_slice.45
  338.6 1.4 bitcast_dynamic-update-slice_fusion.2
  340.7 1.8 bitcast_add_fusion.5
  342.5 2.4 copy.90
  344.9 1.6 fusion.63
  346.6 2.4 bitcast_add_fusion.2
  349.0 1.4 copy.91
  350.9 1.2 copy-done.2
  352.2 3.7 multiply_reduce_fusion
  355.9 29.0 %psum.7 = f32[1024]{0:T(1024)S(1)} all-reduce(f32[1024]{0:T(1024)S(1)} %get-tuple-element.165), channel_id=1, replica_groups=mesh['sx'=4,'sz'=8,'tp'=8] {'tp'}, use_global_device_ids=true, to_apply=%region_9.10 | all-reduce | flops 1024 | bytes 8192 | tf_op jit(solution)/shard_map/psum | solution.py:155
  384.9 7.9 %fusion.25 = f32[1024,2048]{0,1:T(8,128)} fusion(bf16[512,2048]{0,1:T(8,128)(2,1)} %all-gather.11.cloned.1.call-done, f32[1024,512]{0,1:T(8,128)} %get-tuple-element.166, f32[512]{0:T(512)S(1)} %copy-done.20, f32[1024]{0:T(1024)S(1)} %add_rsqrt_fusion), kind=kOutput, calls=%fused_computation.46 | convolution fusion | flops 2149056512 | bytes 12589056 | tf_op jit(solution)/shard_map/dot_general | solution.py:158
  393.8 47.0 %reduce-scatter.2.cloned.1.call-done = f32[1024,256]{0,1:T(8,128)} async-done(((f32[1024,2048]{0,1:T(8,128)}), f32[1024,256]{0,1:T(8,128)}) %reduce-scatter.2.cloned.1.call-update) | async-done | bytes 1048592 | tf_op jit(solution)/shard_map/reduce_scatter | solution.py:165
  440.8 1.3 select_convert_fusion
  (150 shorter events, 26.1 us)
Async XLA Ops:
  6.5 42.3 %copy-start.25 = (s32[128]{0:T(128)S(1)}, s32[128]{0:T(128)}, u32[]{:S(2)}) copy-start(s32[128]{0:T(128)} %param.28) | copy-start | bytes 1540
  6.5 43.0 %copy-start.24 = (f32[8]{0:T(128)S(1)}, f32[8]{0:T(128)}, u32[]{:S(2)}) copy-start(f32[8]{0:T(128)} %param.23) | copy-start | bytes 100
  6.5 43.1 %copy-start.19 = (f32[4,256]{1,0:T(4,128)S(1)}, f32[4,256]{1,0:T(4,128)}, u32[]{:S(2)}) copy-start(f32[4,256]{1,0:T(4,128)} %param.22) | copy-start | bytes 12292
  6.5 43.2 %copy-start.18 = (f32[4,512]{1,0:T(4,128)S(1)}, f32[4,512]{1,0:T(4,128)}, u32[]{:S(2)}) copy-start(f32[4,512]{1,0:T(4,128)} %param.21) | copy-start | bytes 24580
  6.5 42.2 %all-gather.5.cloned.1.call-start = ((), (), s32[]{:S(2)}) async-start(), calls=%async_computation.1 | async-start | bytes 1622016 | tf_op jit(solution)/shard_map/all_gather | solution.py:74
  9.8 82.1 %all-gather.9.cloned.1.call-start = ((), (), s32[]{:S(2)}) async-start(), calls=%async_computation.3 | async-start | bytes 4718592 | tf_op jit(solution)/shard_map/all_gather | solution.py:68
  10.5 147.4 %all-gather.7.cloned.1.call-start = ((), (), s32[]{:S(2)}) async-start(), calls=%async_computation.2 | async-start | bytes 7208960 | tf_op jit(solution)/shard_map/all_gather | solution.py:73
  48.8 336.2 %all-gather.11.cloned.1.call-start = ((), (), s32[]{:S(2)}) async-start(), calls=%async_computation.4 | async-start | bytes 2621440 | tf_op jit(solution)/shard_map/all_gather | solution.py:160
  49.0 0.5 copy-start.28
  49.7 128.1 %copy-start.22 = (f32[4]{0:T(128)}, f32[4]{0:T(128)S(1)}, u32[]{:S(2)}) copy-start(f32[4]{0:T(128)S(1)} %compare_select_fusion.1) | copy-start | bytes 52
  49.7 135.6 %copy-start.9 = (pred[1024]{0:T(1024)(128)(4,1)}, pred[1024]{0:T(1024)(128)(4,1)S(1)}, u32[]{:S(2)}) copy-start(pred[1024]{0:T(1024)(128)(4,1)S(1)} %get-tuple-element.181) | copy-start | bytes 3076
  49.7 135.6 %copy-start.11 = (pred[1024]{0:T(1024)(128)(4,1)}, pred[1024]{0:T(1024)(128)(4,1)S(1)}, u32[]{:S(2)}) copy-start(pred[1024]{0:T(1024)(128)(4,1)S(1)} %get-tuple-element.182) | copy-start | bytes 3076
  49.7 135.6 %copy-start.13 = (pred[1024]{0:T(1024)(128)(4,1)}, pred[1024]{0:T(1024)(128)(4,1)S(1)}, u32[]{:S(2)}) copy-start(pred[1024]{0:T(1024)(128)(4,1)S(1)} %get-tuple-element.183) | copy-start | bytes 3076
  49.7 135.6 %copy-start.15 = (pred[1024]{0:T(1024)(128)(4,1)}, pred[1024]{0:T(1024)(128)(4,1)S(1)}, u32[]{:S(2)}) copy-start(pred[1024]{0:T(1024)(128)(4,1)S(1)} %get-tuple-element.184) | copy-start | bytes 3076
  49.8 124.4 %copy-start.23 = (f32[8]{0:T(128)S(1)}, f32[8]{0:T(128)}, u32[]{:S(2)}) copy-start(f32[8]{0:T(128)} %param.24) | copy-start | bytes 100
  167.6 6.6 %copy-start.1 = (bf16[1024,1288]{0,1:T(8,128)(2,1)}, bf16[1024,1288]{0,1:T(8,128)(2,1)S(1)}, u32[]{:S(2)}) copy-start(bf16[1024,1288]{0,1:T(8,128)(2,1)S(1)} %fusion.10) | copy-start | bytes 7913476
  167.8 15.7 %collective-permute-start = (bf16[3,512]{0,1:T(8,128)(2,1)S(1)}, bf16[3,512]{0,1:T(8,128)(2,1)S(1)}, u32[]{:S(2)}, u32[]{:S(2)}) collective-permute-start(bf16[3,512]{0,1:T(8,128)(2,1)S(1)} %slice.158), channel_id=1, source_target_pairs={{0,8},{8,16},{16,24},{24,32},{32,40},{40,48},{48,56},{56,64},{64,7... | collective-permute-start | bytes 9224 | tf_op jit(solution)/shard_map/ppermute | solution.py:16
  171.0 9.1 %collective-permute-start.1 = (bf16[3,256]{0,1:T(8,128)(2,1)S(1)}, bf16[3,256]{0,1:T(8,128)(2,1)S(1)}, u32[]{:S(2)}, u32[]{:S(2)}) collective-permute-start(bf16[3,256]{0,1:T(8,128)(2,1)S(1)} %slice.167), channel_id=1, source_target_pairs={{0,8},{8,16},{16,24},{24,32},{32,40},{40,48},{48,56},{56,64},{64,7... | collective-permute-start | bytes 4616 | tf_op jit(solution)/shard_map/ppermute | solution.py:16
  174.3 5.8 %slice-start = ((bf16[1024,1288]{0,1:T(8,128)(2,1)}), bf16[1024,256]{0,1:T(8,128)(2,1)S(1)}, s32[]{:S(2)}) async-start(bf16[1024,1288]{0,1:T(8,128)(2,1)} %copy-done.1), calls=%async_computation.6 | async-start | bytes 1048576 | tf_op jit(solution)/shard_map/slice | solution.py:80
  177.7 2.7 copy-start.8
  201.1 13.0 %collective-permute-start.2 = (f32[8,129,64]{1,2,0:T(8,128)S(1)}, f32[8,129,64]{1,2,0:T(8,128)S(1)}, u32[]{:S(2)}, u32[]{:S(2)}) collective-permute-start(f32[8,129,64]{1,2,0:T(8,128)S(1)} %pad_maximum_fusion), channel_id=1, source_target_pairs={{0,8},{8,16},{16,24},{24,32},{32,40},{40,48},{48,56},{56,64},{64,7... | collective-permute-start | bytes 792584 | tf_op jit(solution)/shard_map/ppermute | solution.py:16
  214.1 13.4 %collective-permute-start.3 = (f32[8,129,64]{1,2,0:T(8,128)S(1)}, f32[8,129,64]{1,2,0:T(8,128)S(1)}, u32[]{:S(2)}, u32[]{:S(2)}) collective-permute-start(f32[8,129,64]{1,2,0:T(8,128)S(1)} %collective-permute-done.2), channel_id=1, source_target_pairs={{0,8},{8,16},{16,24},{24,32},{32,40},{40,48},{48,56},{56,64},{64,7... | collective-permute-start | bytes 792584 | tf_op jit(solution)/shard_map/ppermute | solution.py:16
  227.6 38.5 %copy-start.6 = (bf16[512,64]{0,1:T(8,128)(2,1)S(1)}, bf16[512,64]{0,1:T(8,128)(2,1)}, u32[]{:S(2)}) copy-start(bf16[512,64]{0,1:T(8,128)(2,1)} %param.27) | copy-start | bytes 196612
  227.7 79.2 %copy-start.21 = (f32[8]{0:T(128)S(1)}, f32[8]{0:T(128)}, u32[]{:S(2)}) copy-start(f32[8]{0:T(128)} %param.25) | copy-start | bytes 100
  227.7 27.5 %collective-permute-start.4 = (f32[8,129,64]{1,2,0:T(8,128)S(1)}, f32[8,129,64]{1,2,0:T(8,128)S(1)}, u32[]{:S(2)}, u32[]{:S(2)}) collective-permute-start(f32[8,129,64]{1,2,0:T(8,128)S(1)} %pad_maximum_fusion.1), channel_id=1, source_target_pairs={{0,16},{8,24},{16,32},{24,40},{32,48},{40,56},{48,64},{56,72},{64,... | collective-permute-start | bytes 792584 | tf_op jit(solution)/shard_map/ppermute | solution.py:16
  255.3 0.7 copy-start.4
  256.8 52.8 %collective-permute-start.5 = (f32[8,129,64]{1,2,0:T(8,128)}, f32[8,129,64]{1,2,0:T(8,128)}, u32[]{:S(2)}, u32[]{:S(2)}) collective-permute-start(f32[8,129,64]{1,2,0:T(8,128)} %pad_maximum_fusion.2), channel_id=1, source_target_pairs={{0,32},{8,40},{16,48},{24,56},{32,64},{40,72},{48,80},{56,88},{64,... | collective-permute-start | bytes 792584 | tf_op jit(solution)/shard_map/ppermute | solution.py:16
  306.8 134.0 %reduce-scatter.2.cloned.1.call-start = ((), (), s32[]{:S(2)}) async-start(), calls=%async_computation.5 | async-start | bytes 9437184 | tf_op jit(solution)/shard_map/reduce_scatter | solution.py:165
  308.7 13.1 %copy-start.3 = (bf16[1024,128]{1,0:T(8,128)(2,1)}, bf16[1024,128]{1,0:T(8,128)(2,1)S(1)}, u32[]{:S(2)}) copy-start(bf16[1024,128]{1,0:T(8,128)(2,1)S(1)} %copy.96) | copy-start | bytes 786436
  311.8 9.9 %collective-permute-start.6 = (f32[8,129,64]{1,2,0:T(8,128)S(1)}, f32[8,129,64]{1,2,0:T(8,128)S(1)}, u32[]{:S(2)}, u32[]{:S(2)}) collective-permute-start(f32[8,129,64]{1,2,0:T(8,128)S(1)} %pad_maximum_fusion.3), channel_id=1, source_target_pairs={{0,64},{8,72},{16,80},{24,88},{32,96},{40,104},{48,112},{56,120},{... | collective-permute-start | bytes 792584 | tf_op jit(solution)/shard_map/ppermute | solution.py:16
  342.5 4.1 copy-start
  344.9 1.7 copy-start.5
  344.9 1.7 copy-start.7
  350.4 1.7 copy-start.2
  350.4 1.7 copy-start.10
  350.4 1.7 copy-start.12
  350.4 1.7 copy-start.14
  350.4 1.7 copy-start.16
  350.4 1.7 copy-start.17
  352.2 32.8 %copy-start.20 = (f32[512]{0:T(512)S(1)}, f32[512]{0:T(512)}, u32[]{:S(2)}) copy-start(f32[512]{0:T(512)} %param.26) | copy-start | bytes 6148
  392.9 0.7 copy-start.26
  392.9 0.7 copy-start.27
  392.9 0.8 copy-start.29
Sparse Core Ops, SparseCore 0:
  9.9 38.8 all-gather.4
  50.6 41.3 all-gather.8
  93.7 64.1 all-gather.6
  306.9 37.4 all-gather.10
  393.0 47.7 reduce-scatter.1
where the time goes:
time: 451 us; the launch traced here: 450 us
  waiting for transfers between devices  238 us (53%)
  blocking collectives  69.7 us (15%)
  other arithmetic  37.5 us (8%)
  starting transfers between devices  33.5 us (7%)
  local copies, waits for them, and re-layouts  28.8 us (6%)
  matrix products  27.8 us (6%)
  between operations  13.8 us (3%)
    all_gather x1, waiting for transfers between devices, on_device(): lax.all_gather(lax.all_gather(joined, 'sz', axis=0, tiled=True), 'sx', ax...  66 us
    reduce_scatter x1, waiting for transfers between devices, on_device(): lax.psum_scatter(partial_out, 'tp', scatter_dimension=1, tiled=True)  47 us
    ppermute x7, waiting for transfers between devices, passed_along(): return lax.ppermute(value, axis, pairs)  44.4 us
    all_gather x1, waiting for transfers between devices, on_device(): whole = lax.all_gather(tokens, 'tp', axis=1, tiled=True)  42.1 us
    all_gather x1, blocking collectives, on_device(): lax.all_gather(w_output, 'sz', axis=1, tiled=True)  40.6 us
    all_gather x1, waiting for transfers between devices, on_device(): lax.all_gather(joined, 'sz', axis=0, tiled=True)  38.2 us
    ppermute x7, starting transfers between devices, passed_along(): return lax.ppermute(value, axis, pairs)  33.3 us
    psum x1, blocking collectives, on_device(): squares = lax.psum(jnp.sum(gated * gated, axis=1), 'tp')  29 us
  transfers between devices with their start and end apart: 12, of which 8 were waited for; matrix products, arithmetic and copies ran while one was open for 11% of the time, Pallas kernels for 0%

commit v1 on v0

--- a/solution.py
+++ b/solution.py
@@ -65,7 +65,16 @@
     local_valid = lax.dynamic_slice_in_dim(valid_rows, seq_index * local_blocks, local_blocks)
     in_block = jnp.arange(row_count, dtype=jnp.int32) % BLOCK
     carry_on = jnp.repeat(local_start == 0, BLOCK)
-    whole = lax.all_gather(tokens, "tp", axis=1, tiled=True)
+    ways = lax.axis_size("tp")
+    up = [(d, (d + 1) % ways) for d in range(ways)]
+    down = [(d, (d - 1) % ways) for d in range(ways)]
+    earlier_2, later = ([tokens], [tokens])
+    for __2 in range(ways // 2):
+        earlier_2.append(lax.ppermute(earlier_2[-1], "tp", up))
+    for __2 in range((ways - 1) // 2):
+        later.append(lax.ppermute(later[-1], "tp", down))
+    line = jnp.concatenate([*earlier_2[::-1], *later[1:]], axis=1)
+    whole = jnp.roll(line, (lax.axis_index("tp") - ways // 2) * tokens.shape[1], axis=1)
     local_rows = w_inner.shape[0]
     joined = jnp.concatenate(
         [w_inner.reshape(local_rows, 2 * inner_here), w_states, w_step], axis=1

time: 451 us -> 411 us (0.911)
  waiting for transfers between devices: 238 us -> 167 us
  starting transfers between devices: 33.5 us -> 50.5 us
  local copies, waits for them, and re-layouts: 28.8 us -> 43.2 us
    all_gather x1, waiting for transfers between devices: 66 us -> 16 us  [on_device(): lax.all_gather(lax.all_gather(joined, 'sz', axis=0, tiled=True), 'sx', ax...]
    all_gather x1 -> x0, waiting for transfers between devices: 42.1 us -> none  [on_device(): whole = lax.all_gather(tokens, 'tp', axis=1, tiled=True)]
    ppermute x0 -> x7, waiting for transfers between devices: none -> 20.6 us  [the longest x4 19.8 us: on_device(): earlier_2.append(lax.ppermute(earlier_2[-1], 'tp', up))]
    ppermute x0 -> x7, starting transfers between devices: none -> 16.8 us  [the longest x4 13.5 us: on_device(): earlier_2.append(lax.ppermute(earlier_2[-1], 'tp', up))]
    unnamed x65 -> x80, local copies, waits for them, and re-layouts: 5.18 us -> 18.7 us
  transfers between devices with their start and end apart: 12 -> 18, of which waited for: 8 -> 13; matrix products, arithmetic and copies ran while one was open for 11% -> 15% of each run, Pallas kernels for 0% -> 0%
where the time goes in v1:
time: 411 us; the launch traced here: 410 us
  waiting for transfers between devices  167 us (41%)
  blocking collectives  69.8 us (17%)
  starting transfers between devices  50.5 us (12%)
  local copies, waits for them, and re-layouts  43.2 us (11%)
  other arithmetic  38.6 us (9%)
  matrix products  26.3 us (6%)
  between operations  13.7 us (3%)
    reduce_scatter x1, waiting for transfers between devices, on_device(): lax.psum_scatter(partial_out, 'tp', scatter_dimension=1, tiled=True)  47.1 us
    ppermute x7, waiting for transfers between devices, passed_along(): return lax.ppermute(value, axis, pairs)  44.6 us
    all_gather x1, blocking collectives, on_device(): lax.all_gather(w_output, 'sz', axis=1, tiled=True)  40.4 us
    all_gather x1, waiting for transfers between devices, on_device(): lax.all_gather(joined, 'sz', axis=0, tiled=True)  38.9 us
    ppermute x7, starting transfers between devices, passed_along(): return lax.ppermute(value, axis, pairs)  33.3 us
    psum x1, blocking collectives, on_device(): squares = lax.psum(jnp.sum(gated * gated, axis=1), 'tp')  29.4 us
    ppermute x4, waiting for transfers between devices, on_device(): earlier_2.append(lax.ppermute(earlier_2[-1], 'tp', up))  19.8 us
    unnamed x80, local copies, waits for them, and re-layouts  18.7 us
  transfers between devices with their start and end apart: 18, of which 13 were waited for; matrix products, arithmetic and copies ran while one was open for 15% of the time, Pallas kernels for 0%

profile of v1, /device:TPU:1, one launch (start us, length us, event | category | flops | bytes accessed | tf_op | source)
XLA Modules:
  0.0 409.6 jit_solution(5529282127130745406)
XLA Ops:
  8.3 1.4 pad_maximum_fusion.4
  9.9 38.9 %all-gather.4.cloned.1.call-done = bf16[512,1288]{1,0:T(8,128)(2,1)} async-done(((bf16[64,1288]{1,0:T(8,128)(2,1)}), bf16[512,1288]{1,0:T(8,128)(2,1)}) %all-gather.4.cloned.1.call-update) | async-done | bytes 1318928 | tf_op jit(solution)/shard_map/all_gather | solution.py:83
  48.9 6.1 %collective-permute-start = (bf16[1024,256]{1,0:T(8,128)(2,1)S(1)}, bf16[1024,256]{1,0:T(8,128)(2,1)S(1)}, u32[]{:S(2)}, u32[]{:S(2)}) collective-permute-start(bf16[1024,256]{1,0:T(8,128)(2,1)S(1)} %copy-done.2), channel_id=1, source_target_pairs={{0,1},{1,2},{2,3},{3,4},{4,5},{5,6},{6,7},{7,0},{8,9},{9,10},{10,1... | collective-permute-start | bytes 1572872 | tf_op jit(solution)/shard_map/ppermute | solution.py:73
  54.9 6.1 %collective-permute-done = bf16[1024,256]{1,0:T(8,128)(2,1)S(1)} collective-permute-done((bf16[1024,256]{1,0:T(8,128)(2,1)S(1)}, bf16[1024,256]{1,0:T(8,128)(2,1)S(1)}, u32[]{:S(2)}, u32[]{:S(2)}) %collective-permute-start) | collective-permute-done | bytes 524320 | tf_op jit(solution)/shard_map/ppermute | solution.py:73
  61.1 2.5 collective-permute-start.1
  63.9 5.8 %collective-permute-done.1 = bf16[1024,256]{1,0:T(8,128)(2,1)S(1)} collective-permute-done((bf16[1024,256]{1,0:T(8,128)(2,1)S(1)}, bf16[1024,256]{1,0:T(8,128)(2,1)S(1)}, u32[]{:S(2)}, u32[]{:S(2)}) %collective-permute-start.1) | collective-permute-done | bytes 524320 | tf_op jit(solution)/shard_map/ppermute | solution.py:73
  69.7 2.5 collective-permute-start.2
  73.8 4.5 %collective-permute-done.2 = bf16[1024,256]{1,0:T(8,128)(2,1)S(1)} collective-permute-done((bf16[1024,256]{1,0:T(8,128)(2,1)S(1)}, bf16[1024,256]{1,0:T(8,128)(2,1)S(1)}, u32[]{:S(2)}, u32[]{:S(2)}) %collective-permute-start.2) | collective-permute-done | bytes 524320 | tf_op jit(solution)/shard_map/ppermute | solution.py:73
  78.3 2.5 collective-permute-start.3
  81.6 2.0 collective-permute-start.6
  83.5 3.3 collective-permute-done.3
  101.1 16.0 %all-gather.6.cloned.1.call-done = bf16[2048,1288]{1,0:T(8,128)(2,1)} async-done(((bf16[512,1288]{1,0:T(8,128)(2,1)}), bf16[2048,1288]{1,0:T(8,128)(2,1)}) %all-gather.6.cloned.1.call-update) | async-done | bytes 5275664 | tf_op jit(solution)/shard_map/all_gather | solution.py:82
  117.1 9.3 %fusion.12 = bf16[1024,1288]{0,1:T(8,128)(2,1)S(1)} fusion(bf16[2048,1288]{1,0:T(8,128)(2,1)} %all-gather.6.cloned.1.call-done, bf16[1024,4096]{1,0:T(8,128)(2,1)} %constant_dynamic-update-slice_fusion, s32[]{:T(128)S(6)} %select_n.101), kind=kOutput, calls=%fused_computation.21 | convolution fusion | flops 5403582464 | bytes 12599300 | tf_op jit(solution)/shard_map/dot_general | solution.py:85
  128.0 3.2 collective-permute-start.8
  131.2 3.2 collective-permute-start.7
  134.5 2.3 reduce-window.6
  142.5 1.8 maximum_convert_fusion
  144.3 3.1 multiply_convert_fusion.5
  147.4 2.7 reshape.134
  150.0 4.9 %fusion.19 = f32[4,8,128,64]{3,2,1,0:T(8,128)} fusion(f32[4,256,128]{2,1,0:T(8,128)} %copy.83, f32[4,256,8]{1,2,0:T(8,128)S(1)} %exponential_multiply_fusion, bf16[4,256,8,64]{1,0,3,2:T(4,128)(2,1)} %reshape.134), kind=kOutput, calls=%fused_computation.28 | convolution fusion | flops 136314880 | bytes 2654208 | tf_op jit(solution)/shard_map/cjhn,cjhp->chnp/dot_general | solution.py:116
  155.0 4.8 %while.26 = (s32[]{:T(128)}, f32[8]{0:T(128)S(1)}, f32[8,128,64]{2,1,0:T(8,128)S(1)}, f32[4,8]{1,0:T(4,128)S(1)}, f32[4,8,128,64]{3,2,1,0:T(8,128)}, /*index=5*/s32[]{:T(128)}, s32[]{:T(128)}) while((s32[]{:T(128)}, f32[8]{0:T(128)S(1)}, f32[8,128,64]{2,1,0:T(8,128)S(1)}, f32[4,8]{1,0:T(4,128)S(1)}, f32[4,8,128,64]{3,2,1,0:T(8,128)}, ...), condition=%wide.region_5.6_spmd.clone, body=%wide.region_4.5_spmd.clone.sunk | while | flops 196627 | bytes 786688 | solution.py:126
  161.2 3.2 collective-permute-start.9
  164.5 9.8 %collective-permute-done.9 = f32[8,129,64]{1,2,0:T(8,128)S(1)} collective-permute-done((f32[8,129,64]{1,2,0:T(8,128)S(1)}, f32[8,129,64]{1,2,0:T(8,128)S(1)}, u32[]{:S(2)}, u32[]{:S(2)}) %collective-permute-start.9) | collective-permute-done | bytes 264224 | tf_op jit(solution)/shard_map/ppermute | solution.py:16
  174.3 4.4 %collective-permute-start.10 = (f32[8,129,64]{1,2,0:T(8,128)S(1)}, f32[8,129,64]{1,2,0:T(8,128)S(1)}, u32[]{:S(2)}, u32[]{:S(2)}) collective-permute-start(f32[8,129,64]{1,2,0:T(8,128)S(1)} %collective-permute-done.9), channel_id=1, source_target_pairs={{0,8},{8,16},{16,24},{24,32},{32,40},{40,48},{48,56},{56,64},{64,7... | collective-permute-start | bytes 792584 | tf_op jit(solution)/shard_map/ppermute | solution.py:16
  178.9 8.8 %collective-permute-done.10 = f32[8,129,64]{1,2,0:T(8,128)S(1)} collective-permute-done((f32[8,129,64]{1,2,0:T(8,128)S(1)}, f32[8,129,64]{1,2,0:T(8,128)S(1)}, u32[]{:S(2)}, u32[]{:S(2)}) %collective-permute-start.10) | collective-permute-done | bytes 264224 | tf_op jit(solution)/shard_map/ppermute | solution.py:16
  188.0 6.1 %collective-permute-start.11 = (f32[8,129,64]{1,2,0:T(8,128)S(1)}, f32[8,129,64]{1,2,0:T(8,128)S(1)}, u32[]{:S(2)}, u32[]{:S(2)}) collective-permute-start(f32[8,129,64]{1,2,0:T(8,128)S(1)} %pad_maximum_fusion.1), channel_id=1, source_target_pairs={{0,16},{8,24},{16,32},{24,40},{32,48},{40,56},{48,64},{56,72},{64,... | collective-permute-start | bytes 792584 | tf_op jit(solution)/shard_map/ppermute | solution.py:16
  194.2 21.3 %collective-permute-done.11 = f32[8,129,64]{1,2,0:T(8,128)S(1)} collective-permute-done((f32[8,129,64]{1,2,0:T(8,128)S(1)}, f32[8,129,64]{1,2,0:T(8,128)S(1)}, u32[]{:S(2)}, u32[]{:S(2)}) %collective-permute-start.11) | collective-permute-done | bytes 264224 | tf_op jit(solution)/shard_map/ppermute | solution.py:16
  217.1 9.3 %collective-permute-start.12 = (f32[8,129,64]{1,2,0:T(8,128)}, f32[8,129,64]{1,2,0:T(8,128)}, u32[]{:S(2)}, u32[]{:S(2)}) collective-permute-start(f32[8,129,64]{1,2,0:T(8,128)} %pad_maximum_fusion.2), channel_id=1, source_target_pairs={{0,32},{8,40},{16,48},{24,56},{32,64},{40,72},{48,80},{56,88},{64,... | collective-permute-start | bytes 792584 | tf_op jit(solution)/shard_map/ppermute | solution.py:16
  226.4 40.4 %all_gather.14 = bf16[512,512]{0,1:T(8,128)(2,1)} all-gather(bf16[512,64]{0,1:T(8,128)(2,1)S(1)} %copy-done.5), channel_id=1, replica_groups=mesh['sx'=4,'sz'=8,'tp'=8] {'sz'}, dimensions={1}, use_global_device_ids=true | all-gather | bytes 589824 | tf_op jit(solution)/shard_map/all_gather | solution.py:170
  272.0 4.0 collective-permute-start.13
  277.4 4.6 %collective-permute-done.13 = f32[8,129,64]{1,2,0:T(8,128)S(1)} collective-permute-done((f32[8,129,64]{1,2,0:T(8,128)S(1)}, f32[8,129,64]{1,2,0:T(8,128)S(1)}, u32[]{:S(2)}, u32[]{:S(2)}) %collective-permute-start.13) | collective-permute-done | bytes 264224 | tf_op jit(solution)/shard_map/ppermute | solution.py:16
  282.4 20.5 %while.25 = (s32[]{:T(128)}, f32[8,128,64]{2,1,0:T(8,128)S(1)}, bf16[4,8,128,64]{3,2,1,0:T(8,128)(2,1)}, f32[4,8]{1,0:T(4,128)}, f32[4]{0:T(128)}, /*index=5*/f32[4,8,128,64]{3,2,1,0:T(8,128)}, s32[]{:T(128)}) while((s32[]{:T(128)}, f32[8,128,64]{2,1,0:T(8,128)S(1)}, bf16[4,8,128,64]{3,2,1,0:T(8,128)(2,1)}, f32[4,8]{1,0:T(4,128)}, ...), condition=%wide.region_7.8_spmd, body=%wide.region_6.7_spmd.sunk | while | flops 262146 | bytes 1574085 | solution.py:155
  283.6 1.4 bitcast_dynamic-update-slice_fusion.2
  285.7 1.8 bitcast_add_fusion.5
  288.8 1.4 bitcast_dynamic-update-slice_fusion.2
  290.8 1.8 bitcast_add_fusion.5
  293.9 1.4 bitcast_dynamic-update-slice_fusion.2
  296.0 1.8 bitcast_add_fusion.5
  299.0 1.4 bitcast_dynamic-update-slice_fusion.2
  301.1 1.8 bitcast_add_fusion.5
  302.9 1.6 copy.90
  306.1 2.4 bitcast_add_fusion.2
  308.5 1.4 copy.91
  310.6 4.7 %multiply_reduce_fusion = (f32[1024]{0:T(1024)S(1)}, f32[1024,512]{0,1:T(8,128)}) fusion(bf16[1024,1288]{0,1:T(8,128)(2,1)} %copy-done.1, f32[1024,512]{0,1:T(8,128)S(1)} %bitcast.75, f32[512]{0:T(512)S(1)} %copy-done.17, f32[512]{0:T(512)S(1)} %bitcast.91, f32[1027,512]{0,1:T(8,128)S(1)} %maximum_convert_fusion, pred[1024]{0:T(1024)(128)(4,1)S(1)} %copy-done.12, ...), kind=kLoop, calls=%fused_computation.42 | loop fusion | flops 14154752 | bytes 13649920 | tf_op jit(solution)/shard_map/reduce_sum | solution.py:164
  315.3 29.4 %psum.7 = f32[1024]{0:T(1024)S(1)} all-reduce(f32[1024]{0:T(1024)S(1)} %get-tuple-element.165), channel_id=1, replica_groups=mesh['sx'=4,'sz'=8,'tp'=8] {'tp'}, use_global_device_ids=true, to_apply=%region_9.10 | all-reduce | flops 1024 | bytes 8192 | tf_op jit(solution)/shard_map/psum | solution.py:164
  344.8 7.9 %fusion.29 = f32[1024,2048]{0,1:T(8,128)} fusion(bf16[512,2048]{0,1:T(8,128)(2,1)} %all-gather.8.cloned.1.call-done, f32[1024,512]{0,1:T(8,128)} %get-tuple-element.166, f32[512]{0:T(512)S(1)} %copy-done.20, f32[1024]{0:T(1024)S(1)} %add_rsqrt_fusion), kind=kOutput, calls=%fused_computation.47 | convolution fusion | flops 2149056512 | bytes 12589056 | tf_op jit(solution)/shard_map/dot_general | solution.py:167
  353.6 47.1 %reduce-scatter.2.cloned.1.call-done = f32[1024,256]{0,1:T(8,128)} async-done(((f32[1024,2048]{0,1:T(8,128)}), f32[1024,256]{0,1:T(8,128)}) %reduce-scatter.2.cloned.1.call-update) | async-done | bytes 1048592 | tf_op jit(solution)/shard_map/reduce_scatter | solution.py:174
  400.7 1.3 select_convert_fusion
  (176 shorter events, 53.1 us)
Async XLA Ops:
  6.5 42.3 %copy-start.2 = (bf16[1024,256]{1,0:T(8,128)(2,1)S(1)}, bf16[1024,256]{1,0:T(8,128)(2,1)}, u32[]{:S(2)}) copy-start(bf16[1024,256]{1,0:T(8,128)(2,1)} %param.17) | copy-start | bytes 1572868
  6.5 57.1 %copy-start.25 = (s32[128]{0:T(128)S(1)}, s32[128]{0:T(128)}, u32[]{:S(2)}) copy-start(s32[128]{0:T(128)} %param.28) | copy-start | bytes 1540
  6.5 65.8 %copy-start.24 = (f32[8]{0:T(128)S(1)}, f32[8]{0:T(128)}, u32[]{:S(2)}) copy-start(f32[8]{0:T(128)} %param.23) | copy-start | bytes 100
  6.5 74.3 %copy-start.19 = (f32[4,256]{1,0:T(4,128)S(1)}, f32[4,256]{1,0:T(4,128)}, u32[]{:S(2)}) copy-start(f32[4,256]{1,0:T(4,128)} %param.22) | copy-start | bytes 12292
  6.5 74.3 %copy-start.18 = (f32[4,512]{1,0:T(4,128)S(1)}, f32[4,512]{1,0:T(4,128)}, u32[]{:S(2)}) copy-start(f32[4,512]{1,0:T(4,128)} %param.21) | copy-start | bytes 24580
  6.5 42.2 %all-gather.4.cloned.1.call-start = ((), (), s32[]{:S(2)}) async-start(), calls=%async_computation.1 | async-start | bytes 1622016 | tf_op jit(solution)/shard_map/all_gather | solution.py:83
  9.8 107.3 %all-gather.6.cloned.1.call-start = ((), (), s32[]{:S(2)}) async-start(), calls=%async_computation.2 | async-start | bytes 7208960 | tf_op jit(solution)/shard_map/all_gather | solution.py:82
  48.8 295.9 %all-gather.8.cloned.1.call-start = ((), (), s32[]{:S(2)}) async-start(), calls=%async_computation.3 | async-start | bytes 2621440 | tf_op jit(solution)/shard_map/all_gather | solution.py:169
  48.9 12.2 %collective-permute-start = (bf16[1024,256]{1,0:T(8,128)(2,1)S(1)}, bf16[1024,256]{1,0:T(8,128)(2,1)S(1)}, u32[]{:S(2)}, u32[]{:S(2)}) collective-permute-start(bf16[1024,256]{1,0:T(8,128)(2,1)S(1)} %copy-done.2), channel_id=1, source_target_pairs={{0,1},{1,2},{2,3},{3,4},{4,5},{5,6},{6,7},{7,0},{8,9},{9,10},{10,1... | collective-permute-start | bytes 1572872 | tf_op jit(solution)/shard_map/ppermute | solution.py:73
  61.1 8.6 %collective-permute-start.1 = (bf16[1024,256]{1,0:T(8,128)(2,1)S(1)}, bf16[1024,256]{1,0:T(8,128)(2,1)S(1)}, u32[]{:S(2)}, u32[]{:S(2)}) collective-permute-start(bf16[1024,256]{1,0:T(8,128)(2,1)S(1)} %collective-permute-done), channel_id=1, source_target_pairs={{0,1},{1,2},{2,3},{3,4},{4,5},{5,6},{6,7},{7,0},{8,9},{9,10},{10,1... | collective-permute-start | bytes 1572872 | tf_op jit(solution)/shard_map/ppermute | solution.py:73
  63.6 9.0 %collective-permute-start.4 = (bf16[1024,256]{1,0:T(8,128)(2,1)S(1)}, bf16[1024,256]{1,0:T(8,128)(2,1)S(1)}, u32[]{:S(2)}, u32[]{:S(2)}) collective-permute-start(bf16[1024,256]{1,0:T(8,128)(2,1)S(1)} %copy-done.2), channel_id=1, source_target_pairs={{0,7},{1,0},{2,1},{3,2},{4,3},{5,4},{6,5},{7,6},{8,15},{9,8},{10,9... | collective-permute-start | bytes 1572872 | tf_op jit(solution)/shard_map/ppermute | solution.py:75
  63.9 8.4 %copy-start.28 = (s32[128]{0:T(128)}, s32[128]{0:T(128)S(1)}, u32[]{:S(2)}) copy-start(s32[128]{0:T(128)S(1)} %select_reduce_fusion) | copy-start | bytes 1540
  69.7 8.6 %collective-permute-start.2 = (bf16[1024,256]{1,0:T(8,128)(2,1)S(1)}, bf16[1024,256]{1,0:T(8,128)(2,1)S(1)}, u32[]{:S(2)}, u32[]{:S(2)}) collective-permute-start(bf16[1024,256]{1,0:T(8,128)(2,1)S(1)} %collective-permute-done.1), channel_id=1, source_target_pairs={{0,1},{1,2},{2,3},{3,4},{4,5},{5,6},{6,7},{7,0},{8,9},{9,10},{10,1... | collective-permute-start | bytes 1572872 | tf_op jit(solution)/shard_map/ppermute | solution.py:73
  72.4 71.9 %copy-start.9 = (pred[1024]{0:T(1024)(128)(4,1)}, pred[1024]{0:T(1024)(128)(4,1)S(1)}, u32[]{:S(2)}) copy-start(pred[1024]{0:T(1024)(128)(4,1)S(1)} %get-tuple-element.181) | copy-start | bytes 3076
  72.4 71.9 %copy-start.11 = (pred[1024]{0:T(1024)(128)(4,1)}, pred[1024]{0:T(1024)(128)(4,1)S(1)}, u32[]{:S(2)}) copy-start(pred[1024]{0:T(1024)(128)(4,1)S(1)} %get-tuple-element.182) | copy-start | bytes 3076
  72.4 71.9 %copy-start.13 = (pred[1024]{0:T(1024)(128)(4,1)}, pred[1024]{0:T(1024)(128)(4,1)S(1)}, u32[]{:S(2)}) copy-start(pred[1024]{0:T(1024)(128)(4,1)S(1)} %get-tuple-element.183) | copy-start | bytes 3076
  72.4 71.9 %copy-start.15 = (pred[1024]{0:T(1024)(128)(4,1)}, pred[1024]{0:T(1024)(128)(4,1)S(1)}, u32[]{:S(2)}) copy-start(pred[1024]{0:T(1024)(128)(4,1)S(1)} %get-tuple-element.184) | copy-start | bytes 3076
  72.6 9.0 %collective-permute-start.5 = (bf16[1024,256]{1,0:T(8,128)(2,1)S(1)}, bf16[1024,256]{1,0:T(8,128)(2,1)S(1)}, u32[]{:S(2)}, u32[]{:S(2)}) collective-permute-start(bf16[1024,256]{1,0:T(8,128)(2,1)S(1)} %collective-permute-done.4), channel_id=1, source_target_pairs={{0,7},{1,0},{2,1},{3,2},{4,3},{5,4},{6,5},{7,6},{8,15},{9,8},{10,9... | collective-permute-start | bytes 1572872 | tf_op jit(solution)/shard_map/ppermute | solution.py:75
  78.3 8.6 %collective-permute-start.3 = (bf16[1024,256]{1,0:T(8,128)(2,1)S(1)}, bf16[1024,256]{1,0:T(8,128)(2,1)S(1)}, u32[]{:S(2)}, u32[]{:S(2)}) collective-permute-start(bf16[1024,256]{1,0:T(8,128)(2,1)S(1)} %collective-permute-done.2), channel_id=1, source_target_pairs={{0,1},{1,2},{2,3},{3,4},{4,5},{5,6},{6,7},{7,0},{8,9},{9,10},{10,1... | collective-permute-start | bytes 1572872 | tf_op jit(solution)/shard_map/ppermute | solution.py:73
  80.8 57.1 %copy-start.22 = (f32[4]{0:T(128)}, f32[4]{0:T(128)S(1)}, u32[]{:S(2)}) copy-start(f32[4]{0:T(128)S(1)} %compare_select_fusion.1) | copy-start | bytes 52
  81.6 11.5 %collective-permute-start.6 = (bf16[1024,256]{1,0:T(8,128)(2,1)S(1)}, bf16[1024,256]{1,0:T(8,128)(2,1)S(1)}, u32[]{:S(2)}, u32[]{:S(2)}) collective-permute-start(bf16[1024,256]{1,0:T(8,128)(2,1)S(1)} %collective-permute-done.5), channel_id=1, source_target_pairs={{0,7},{1,0},{2,1},{3,2},{4,3},{5,4},{6,5},{7,6},{8,15},{9,8},{10,9... | collective-permute-start | bytes 1572872 | tf_op jit(solution)/shard_map/ppermute | solution.py:75
  101.1 33.3 %copy-start.23 = (f32[8]{0:T(128)S(1)}, f32[8]{0:T(128)}, u32[]{:S(2)}) copy-start(f32[8]{0:T(128)} %param.24) | copy-start | bytes 100
  126.4 12.9 %copy-start.1 = (bf16[1024,1288]{0,1:T(8,128)(2,1)}, bf16[1024,1288]{0,1:T(8,128)(2,1)S(1)}, u32[]{:S(2)}) copy-start(bf16[1024,1288]{0,1:T(8,128)(2,1)S(1)} %fusion.12) | copy-start | bytes 7913476
  128.0 11.1 %collective-permute-start.8 = (bf16[3,256]{0,1:T(8,128)(2,1)}, bf16[3,256]{0,1:T(8,128)(2,1)S(1)}, u32[]{:S(2)}, u32[]{:S(2)}) collective-permute-start(bf16[3,256]{0,1:T(8,128)(2,1)} %slice.167), channel_id=1, source_target_pairs={{0,8},{8,16},{16,24},{24,32},{32,40},{40,48},{48,56},{56,64},{64,7... | collective-permute-start | bytes 4616 | tf_op jit(solution)/shard_map/ppermute | solution.py:16
  131.2 11.3 %collective-permute-start.7 = (bf16[3,512]{0,1:T(8,128)(2,1)}, bf16[3,512]{0,1:T(8,128)(2,1)S(1)}, u32[]{:S(2)}, u32[]{:S(2)}) collective-permute-start(bf16[3,512]{0,1:T(8,128)(2,1)} %slice.158), channel_id=1, source_target_pairs={{0,8},{8,16},{16,24},{24,32},{32,40},{40,48},{48,56},{56,64},{64,7... | collective-permute-start | bytes 9224 | tf_op jit(solution)/shard_map/ppermute | solution.py:16
  137.8 1.5 copy-start.8
  159.7 0.5 copy-start.7
  161.2 13.1 %collective-permute-start.9 = (f32[8,129,64]{1,2,0:T(8,128)S(1)}, f32[8,129,64]{1,2,0:T(8,128)S(1)}, u32[]{:S(2)}, u32[]{:S(2)}) collective-permute-start(f32[8,129,64]{1,2,0:T(8,128)S(1)} %pad_maximum_fusion), channel_id=1, source_target_pairs={{0,8},{8,16},{16,24},{24,32},{32,40},{40,48},{48,56},{56,64},{64,7... | collective-permute-start | bytes 792584 | tf_op jit(solution)/shard_map/ppermute | solution.py:16
  174.3 13.4 %collective-permute-start.10 = (f32[8,129,64]{1,2,0:T(8,128)S(1)}, f32[8,129,64]{1,2,0:T(8,128)S(1)}, u32[]{:S(2)}, u32[]{:S(2)}) collective-permute-start(f32[8,129,64]{1,2,0:T(8,128)S(1)} %collective-permute-done.9), channel_id=1, source_target_pairs={{0,8},{8,16},{16,24},{24,32},{32,40},{40,48},{48,56},{56,64},{64,7... | collective-permute-start | bytes 792584 | tf_op jit(solution)/shard_map/ppermute | solution.py:16
  187.8 38.6 %copy-start.5 = (bf16[512,64]{0,1:T(8,128)(2,1)S(1)}, bf16[512,64]{0,1:T(8,128)(2,1)}, u32[]{:S(2)}) copy-start(bf16[512,64]{0,1:T(8,128)(2,1)} %param.27) | copy-start | bytes 196612
  187.9 79.2 %copy-start.21 = (f32[8]{0:T(128)S(1)}, f32[8]{0:T(128)}, u32[]{:S(2)}) copy-start(f32[8]{0:T(128)} %param.25) | copy-start | bytes 100
  188.0 27.5 %collective-permute-start.11 = (f32[8,129,64]{1,2,0:T(8,128)S(1)}, f32[8,129,64]{1,2,0:T(8,128)S(1)}, u32[]{:S(2)}, u32[]{:S(2)}) collective-permute-start(f32[8,129,64]{1,2,0:T(8,128)S(1)} %pad_maximum_fusion.1), channel_id=1, source_target_pairs={{0,16},{8,24},{16,32},{24,40},{32,48},{40,56},{48,64},{56,72},{64,... | collective-permute-start | bytes 792584 | tf_op jit(solution)/shard_map/ppermute | solution.py:16
  215.5 0.7 copy-start.3
  217.1 52.8 %collective-permute-start.12 = (f32[8,129,64]{1,2,0:T(8,128)}, f32[8,129,64]{1,2,0:T(8,128)}, u32[]{:S(2)}, u32[]{:S(2)}) collective-permute-start(f32[8,129,64]{1,2,0:T(8,128)} %pad_maximum_fusion.2), channel_id=1, source_target_pairs={{0,32},{8,40},{16,48},{24,56},{32,64},{40,72},{48,80},{56,88},{64,... | collective-permute-start | bytes 792584 | tf_op jit(solution)/shard_map/ppermute | solution.py:16
  266.8 133.9 %reduce-scatter.2.cloned.1.call-start = ((), (), s32[]{:S(2)}) async-start(), calls=%async_computation.4 | async-start | bytes 9437184 | tf_op jit(solution)/shard_map/reduce_scatter | solution.py:174
  272.0 10.0 %collective-permute-start.13 = (f32[8,129,64]{1,2,0:T(8,128)S(1)}, f32[8,129,64]{1,2,0:T(8,128)S(1)}, u32[]{:S(2)}, u32[]{:S(2)}) collective-permute-start(f32[8,129,64]{1,2,0:T(8,128)S(1)} %pad_maximum_fusion.3), channel_id=1, source_target_pairs={{0,64},{8,72},{16,80},{24,88},{32,96},{40,104},{48,112},{56,120},{... | collective-permute-start | bytes 792584 | tf_op jit(solution)/shard_map/ppermute | solution.py:16
  302.9 2.1 copy-start.6
  304.5 1.2 copy-start
  304.6 1.5 copy-start.4
  309.9 0.7 copy-start.10
  309.9 0.7 copy-start.12
  309.9 0.7 copy-start.14
  309.9 0.7 copy-start.16
  309.9 0.7 copy-start.17
  310.6 34.2 %copy-start.20 = (f32[512]{0:T(512)S(1)}, f32[512]{0:T(512)}, u32[]{:S(2)}) copy-start(f32[512]{0:T(512)} %param.26) | copy-start | bytes 6148
  352.7 0.7 copy-start.26
  352.7 0.7 copy-start.27
  352.7 0.8 copy-start.29
Sparse Core Ops, SparseCore 0:
  9.9 38.8 all-gather.3
  50.6 66.4 all-gather.5
  267.0 37.6 all-gather.7
  352.9 47.8 reduce-scatter.1
